TPU v7x, 512 devices: a whole 4x4x16 slice. The times are simulated.
512 devices in a mesh: take: 4 (over y), outer: 16 (over z), inner: 8 (over x, core).
Axes of the slice: x: 4, y: 4, z: 16, core: 2. Of those that a mesh axis runs over, the one named last changes fastest.
Arguments:
- frames: bfloat16 [16, 65536, 256], P('take', ('outer', 'inner')), may hold values from -6 to 6
- conv_weight: bfloat16 [3, 3, 256, 256], replicated, may hold values from -0.21875 to 0.21875
- conv_bias: float32 [3, 256], replicated, may hold values from -1 to 1
- dilations: int32 [3], replicated, may hold values from 1 to 64, as said below
- head_weight: bfloat16 [256, 128], replicated, may hold values from -0.375 to 0.375
- present: int32 [16, 65536], P('take', ('outer', 'inner')), may hold values 0 or 1
- frame_keep: float32 [16, 65536], P('take', ('outer', 'inner')), may hold values from 0.5 to 1
- channel_params: float32 [3, 64], replicated, may hold values from 0 to 2
- head_cotangent: bfloat16 [16, 65536, 128], P('take', ('outer', 'inner')), may hold values from -6 to 6
Outputs:
- filtered_mean: float32 [16, 64, 65536], P('take', None, ('outer', 'inner'))
- head_grad: float32 [256, 128], replicated
Inputs may be any that keep to these rules, and one draw needn't show every extreme that they name: `dilations`: every dilation is 1 to 64; some layer has exactly 64 and another exactly 1.
All inputs are finite; a program needn't handle non-finite values. No bound on the sum of `present` on one device may be relied on, other than what follows from the above.
Results may differ from a plain program's by a relative error of at most 0.0048.
Values may be sent and summed in bfloat16 or wider, within the bound.
No kernel may reach another device: no remote copies, remote signals or barrier semaphores. Data moves between devices by JAX's collectives and lax.ppermute only.
A program may use at most 64 MiB of HBM per device.

v0:
```python
import jax
import jax.numpy as jnp
from jax import lax
from jax.sharding import PartitionSpec as P

STATE = 64
LAYERS = 3
DMAX = 64


def extended_2(block, sides, width):
    for axis, dim in sides:
        count = lax.axis_size(axis)
        forward = [(i, i + 1) for i in range(count - 1)]
        backward = [(target, source) for source, target in forward]
        low = lax.ppermute(
            lax.slice_in_dim(block, block.shape[dim] - width, None, axis=dim), axis, forward
        )
        high = lax.ppermute(lax.slice_in_dim(block, 0, width, axis=dim), axis, backward)
        block = jnp.concatenate([low, block, high], axis=dim)
    return block


def prefix_2(part, axis, combine, identity):
    place = lax.axis_index(axis)
    gathered = jax.tree.map(lambda a: lax.all_gather(a, axis), part)
    state = jax.tree.map(lambda a, e: jnp.zeros_like(a) + jnp.asarray(e, a.dtype), part, identity)

    def one(turn, state):
        return combine(
            state, jax.tree.map(lambda a: lax.dynamic_index_in_dim(a, turn, 0, False), gathered)
        )

    return lax.fori_loop(0, place, one, state)


def combine(early, late):
    a_one, b_one, c_one, e_one, j_one = early
    a_two, b_two, c_two, e_two, j_two = late
    denom = 1.0 + c_one * j_two
    new_a = a_two * a_one / denom
    new_b = a_two * (b_one + c_one * e_two) / denom + b_two
    new_c = a_two * a_two * c_one / denom + c_two
    new_e = a_one * (e_two - j_two * b_one) / denom + e_one
    new_j = a_one * a_one * j_two / denom + j_one
    return (new_a, new_b, new_c, new_e, new_j)


def doubling_prefix(elems, axis):
    length = elems[0].shape[axis]
    result = elems
    offset = 1
    while offset < length:
        moved = []
        for index, item in enumerate(result):
            fill_value = 1.0 if index == 0 else 0.0
            pad_shape = list(item.shape)
            pad_shape[axis] = offset
            fill = jnp.full(pad_shape, fill_value, item.dtype)
            kept = lax.slice_in_dim(item, 0, length - offset, axis=axis)
            moved.append(jnp.concatenate([fill, kept], axis=axis))
        result = combine(tuple(moved), result)
        offset = offset * 2
    return result


def exclusive_in_group(totals, axis):
    place = lax.axis_index(axis)
    gathered = lax.all_gather(totals, axis)
    inclusive = doubling_prefix(tuple((gathered[:, k] for k in range(5))), 0)
    inclusive = jnp.stack(inclusive, axis=1)
    earlier = lax.dynamic_index_in_dim(inclusive, jnp.maximum(place - 1, 0), 0, False)
    identity = jnp.zeros_like(earlier).at[0].set(1.0)
    earlier = jnp.where(place > 0, earlier, identity)
    return (earlier, inclusive[-1])


def block_prefix(totals):
    inner_excl, group_total = exclusive_in_group(totals, "inner")
    outer_excl, _ = exclusive_in_group(group_total, "outer")
    return combine(tuple(outer_excl), tuple(inner_excl))


def elements(obs, logp, params, present, keep, first):
    rate = params[0][:, None]
    noise = params[1][:, None]
    scale = params[2][:, None]
    trans = jnp.exp(-rate) * keep
    prec = present * scale * jax.nn.softplus(logp)
    denom = 1.0 + noise * prec
    zeros = jnp.zeros_like(obs)
    elem_a = jnp.where(first, zeros, trans / denom)
    elem_b = jnp.where(first, prec * obs / (1.0 + prec), noise * prec * obs / denom)
    elem_c = jnp.where(first, 1.0 / (1.0 + prec), noise / denom)
    elem_e = jnp.where(first, zeros, trans * prec * obs / denom)
    elem_j = jnp.where(first, zeros, trans * trans * prec / denom)
    return (elem_a, elem_b, elem_c, elem_e, elem_j)


def conv_layer(extended, weights, bias, dilation):
    out_len = extended.shape[1] - 2 * DMAX
    acc = jnp.zeros((extended.shape[0], out_len, extended.shape[2]), jnp.float32)
    for tap in range(3):
        piece = lax.dynamic_slice_in_dim(extended, DMAX + (tap - 1) * dilation, out_len, 1)
        acc = acc + jnp.einsum(
            "tfw,wv->tfv", piece, weights[tap], preferred_element_type=jnp.float32
        )
    center = extended[:, DMAX : DMAX + out_len]
    return (center.astype(jnp.float32) + jax.nn.silu(acc + bias[None, None, :])).astype(
        jnp.bfloat16
    )


def per_device(
    frames,
    conv_weight,
    conv_bias,
    dilations,
    head_weight,
    present,
    frame_keep,
    channel_params,
    head_cotangent,
):
    block_len = frames.shape[1]
    position = lax.axis_index(("outer", "inner"))
    hidden = frames
    for layer in range(LAYERS):
        extended = extended_2(hidden, ((("outer", "inner"), 1),), DMAX)
        hidden = conv_layer(extended, conv_weight[layer], conv_bias[layer], dilations[layer])
    head = jnp.einsum("tfw,ws->tsf", hidden, head_weight, preferred_element_type=jnp.float32)
    obs = head[:, :STATE]
    logp = head[:, STATE:]
    places = position * block_len + jnp.arange(block_len, dtype=jnp.int32)
    first = (places == 0)[None, None, :]
    elems = elements(
        obs,
        logp,
        channel_params,
        present.astype(jnp.float32)[:, None, :],
        frame_keep[:, None, :],
        first,
    )
    local = doubling_prefix(elems, 2)
    totals = jnp.stack([item[:, :, -1] for item in local])
    prefix = block_prefix(totals)
    final = combine(tuple((item[:, :, None] for item in prefix)), local)
    grad_local = jnp.einsum(
        "tfw,tfs->ws", hidden, head_cotangent, preferred_element_type=jnp.float32
    )
    head_grad = lax.psum(grad_local, "inner")
    head_grad = lax.psum(head_grad, "outer")
    head_grad = lax.psum(head_grad, "take")
    return (final[1], head_grad)


def solution(mesh):
    return jax.shard_map(
        per_device,
        mesh=mesh,
        in_specs=(
            P("take", ("outer", "inner"), None),
            P(),
            P(),
            P(),
            P(),
            P("take", ("outer", "inner")),
            P("take", ("outer", "inner")),
            P(),
            P("take", ("outer", "inner"), None),
        ),
        out_specs=(P("take", None, ("outer", "inner")), P()),
        check_vma=False,
    )
```

profile of v0, /device:TPU:2, one launch (start us, length us, event | category | flops | bytes accessed | tf_op | source)
XLA Modules:
  0.0 392.9 jit_solution(5290036489453492107)
XLA Ops:
  8.4 1.9 collective-permute-start.1
  10.3 2.4 collective-permute-start
  14.3 3.0 fusion.60
  25.8 1.1 add_convert_fusion.2
  26.9 3.0 collective-permute-start.2
  30.0 6.3 %collective-permute-start.3 = (bf16[4,64,256]{2,1,0:T(8,128)(2,1)S(1)}, bf16[4,64,256]{2,1,0:T(8,128)(2,1)S(1)}, u32[]{:S(2)}, u32[]{:S(2)}) collective-permute-start(bf16[4,64,256]{2,1,0:T(8,128)(2,1)S(1)} %get-tuple-element.108), channel_id=1, source_target_pairs={{1,0},{2,1},{3,2},{4,3},{5,4},{6,5},{7,6},{8,7},{9,8},{10,9},{11,1... | collective-permute-start | bytes 393224 | tf_op jit(solution)/shard_map/ppermute | solution.py:19
  37.0 1.8 collective-permute-done.3
  40.5 1.9 collective-permute-start.4
  42.4 4.0 %collective-permute-start.5 = (bf16[4,64,256]{2,1,0:T(8,128)(2,1)S(1)}, bf16[4,64,256]{2,1,0:T(8,128)(2,1)S(1)}, u32[]{:S(2)}, u32[]{:S(2)}) collective-permute-start(bf16[4,64,256]{2,1,0:T(8,128)(2,1)S(1)} %get-tuple-element.106), channel_id=1, source_target_pairs={{1,0},{2,1},{3,2},{4,3},{5,4},{6,5},{7,6},{8,7},{9,8},{10,9},{11,1... | collective-permute-start | bytes 393224 | tf_op jit(solution)/shard_map/ppermute | solution.py:19
  46.9 1.8 collective-permute-done.5
  49.2 1.1 add_convert_fusion
  53.3 1.3 divide_add_fusion.12
  54.6 1.3 divide_add_fusion.11
  55.9 1.3 divide_add_fusion.10
  57.2 1.3 divide_add_fusion.9
  58.5 1.3 divide_add_fusion.8
  59.9 1.4 fusion.30
  63.9 13.5 %all-gather = f32[40,4,64]{2,1,0:T(4,128)S(1)} all-gather(f32[5,4,64]{2,1,0:T(4,128)S(1)} %constant_dynamic-update-slice_fusion.3), channel_id=2, replica_groups=mesh['take'=4,'outer'=16,'inner'=8] {'inner'}, dimensions={0}, use_global_device_ids=true | all-gather | bytes 46080 | tf_op jit(solution)/shard_map/all_gather | solution.py:69
  77.9 38.7 %all_gather.11 = f32[16,5,4,64]{3,2,0,1:T(4,128)S(1)} all-gather(f32[1,5,4,64]{3,2,0,1:T(4,128)S(1)} %slice.674), channel_id=1, replica_groups=mesh['take'=4,'outer'=16,'inner'=8] {'outer'}, dimensions={0}, use_global_device_ids=true | all-gather | bytes 87040 | tf_op jit(solution)/shard_map/all_gather | solution.py:69
  116.8 1.1 convolution_bitcast_fusion.1
  118.5 69.9 %all-reduce.84.cloned.1.call-done = f32[256,128]{1,0:T(8,128)} async-done(((f32[256,128]{1,0:T(8,128)}), f32[256,128]{1,0:T(8,128)}) %all-reduce.84.cloned.1.call-update) | async-done | bytes 131088 | tf_op jit(solution)/shard_map/psum | solution.py:151
  188.6 139.9 %all-reduce.86.cloned.1.call-done = f32[256,128]{1,0:T(8,128)} async-done(((f32[256,128]{1,0:T(8,128)}), f32[256,128]{1,0:T(8,128)}) %all-reduce.86.cloned.1.call-update) | async-done | bytes 131088 | tf_op jit(solution)/shard_map/psum | solution.py:152
  329.6 55.2 %all-reduce.88.cloned.1.call-done = f32[256,128]{1,0:T(8,128)} async-done(((f32[256,128]{1,0:T(8,128)}), f32[256,128]{1,0:T(8,128)}) %all-reduce.88.cloned.1.call-update) | async-done | bytes 131088 | tf_op jit(solution)/shard_map/psum | solution.py:153
  384.8 1.6 copy.267
  (121 shorter events, 16.1 us)
Async XLA Ops:
  7.2 109.6 %copy-start = (bf16[4,512,128]{2,1,0:T(8,128)(2,1)S(1)}, bf16[4,512,128]{2,1,0:T(8,128)(2,1)}, u32[]{:S(2)}) copy-start(bf16[4,512,128]{2,1,0:T(8,128)(2,1)} %param.21) | copy-start | bytes 1572868
  7.2 16.9 %copy-start.1 = (bf16[4,512,256]{2,1,0:T(8,128)(2,1)S(1)}, bf16[4,512,256]{2,1,0:T(8,128)(2,1)}, u32[]{:S(2)}) copy-start(bf16[4,512,256]{2,1,0:T(8,128)(2,1)} %param.13) | copy-start | bytes 3145732
  7.2 10.1 %copy-start.8 = (s32[3]{0:T(128)S(1)}, s32[3]{0:T(128)}, u32[]{:S(2)}) copy-start(s32[3]{0:T(128)} %param.16) | copy-start | bytes 40
  7.2 16.8 %copy-start.7 = (s32[4,512]{1,0:T(4,128)S(1)}, s32[4,512]{1,0:T(4,128)}, u32[]{:S(2)}) copy-start(s32[4,512]{1,0:T(4,128)} %param.18) | copy-start | bytes 24580
  7.2 181.3 %all-reduce.84.cloned.1.call-start = ((), (), s32[]{:S(2)}) async-start(), calls=%async_computation | async-start | bytes 262144 | tf_op jit(solution)/shard_map/psum | solution.py:151
  8.4 15.8 %collective-permute-start.1 = (bf16[4,64,256]{2,1,0:T(8,128)(2,1)S(1)}, bf16[4,64,256]{2,1,0:T(8,128)(2,1)S(1)}, u32[]{:S(2)}, u32[]{:S(2)}) collective-permute-start(bf16[4,64,256]{2,1,0:T(8,128)(2,1)S(1)} %get-tuple-element.109), channel_id=1, source_target_pairs={{1,0},{2,1},{3,2},{4,3},{5,4},{6,5},{7,6},{8,7},{9,8},{10,9},{11,1... | collective-permute-start | bytes 393224 | tf_op jit(solution)/shard_map/ppermute | solution.py:19
  10.3 13.8 %collective-permute-start = (bf16[4,64,256]{2,1,0:T(8,128)(2,1)S(1)}, bf16[4,64,256]{2,1,0:T(8,128)(2,1)S(1)}, u32[]{:S(2)}, u32[]{:S(2)}) collective-permute-start(bf16[4,64,256]{2,1,0:T(8,128)(2,1)S(1)} %get-tuple-element.110), channel_id=1, source_target_pairs={{0,1},{1,2},{2,3},{3,4},{4,5},{5,6},{6,7},{7,8},{8,9},{9,10},{10,1... | collective-permute-start | bytes 393224 | tf_op jit(solution)/shard_map/ppermute | solution.py:16
  17.3 6.9 %copy-start.3 = (bf16[3,3,256,256]{3,2,1,0:T(8,128)(2,1)S(1)}, bf16[3,3,256,256]{3,2,1,0:T(8,128)(2,1)}, u32[]{:S(2)}) copy-start(bf16[3,3,256,256]{3,2,1,0:T(8,128)(2,1)} %param.14) | copy-start | bytes 3538948
  24.2 1.6 copy-start.2
  26.9 10.1 %collective-permute-start.2 = (bf16[4,64,256]{2,1,0:T(8,128)(2,1)S(1)}, bf16[4,64,256]{2,1,0:T(8,128)(2,1)S(1)}, u32[]{:S(2)}, u32[]{:S(2)}) collective-permute-start(bf16[4,64,256]{2,1,0:T(8,128)(2,1)S(1)} %get-tuple-element.107), channel_id=1, source_target_pairs={{0,1},{1,2},{2,3},{3,4},{4,5},{5,6},{6,7},{7,8},{8,9},{9,10},{10,1... | collective-permute-start | bytes 393224 | tf_op jit(solution)/shard_map/ppermute | solution.py:16
  30.0 8.8 %collective-permute-start.3 = (bf16[4,64,256]{2,1,0:T(8,128)(2,1)S(1)}, bf16[4,64,256]{2,1,0:T(8,128)(2,1)S(1)}, u32[]{:S(2)}, u32[]{:S(2)}) collective-permute-start(bf16[4,64,256]{2,1,0:T(8,128)(2,1)S(1)} %get-tuple-element.108), channel_id=1, source_target_pairs={{1,0},{2,1},{3,2},{4,3},{5,4},{6,5},{7,6},{8,7},{9,8},{10,9},{11,1... | collective-permute-start | bytes 393224 | tf_op jit(solution)/shard_map/ppermute | solution.py:19
  40.5 6.4 %collective-permute-start.4 = (bf16[4,64,256]{2,1,0:T(8,128)(2,1)S(1)}, bf16[4,64,256]{2,1,0:T(8,128)(2,1)S(1)}, u32[]{:S(2)}, u32[]{:S(2)}) collective-permute-start(bf16[4,64,256]{2,1,0:T(8,128)(2,1)S(1)} %get-tuple-element.105), channel_id=1, source_target_pairs={{0,1},{1,2},{2,3},{3,4},{4,5},{5,6},{6,7},{7,8},{8,9},{9,10},{10,1... | collective-permute-start | bytes 393224 | tf_op jit(solution)/shard_map/ppermute | solution.py:16
  42.4 6.3 %collective-permute-start.5 = (bf16[4,64,256]{2,1,0:T(8,128)(2,1)S(1)}, bf16[4,64,256]{2,1,0:T(8,128)(2,1)S(1)}, u32[]{:S(2)}, u32[]{:S(2)}) collective-permute-start(bf16[4,64,256]{2,1,0:T(8,128)(2,1)S(1)} %get-tuple-element.106), channel_id=1, source_target_pairs={{1,0},{2,1},{3,2},{4,3},{5,4},{6,5},{7,6},{8,7},{9,8},{10,9},{11,1... | collective-permute-start | bytes 393224 | tf_op jit(solution)/shard_map/ppermute | solution.py:19
  49.2 1.2 copy-start.4
  50.4 1.0 copy-start.5
  116.7 1.8 copy-start.6
  118.0 210.6 %all-reduce.86.cloned.1.call-start = ((), (), s32[]{:S(2)}) async-start(), calls=%async_computation.1 | async-start | bytes 262144 | tf_op jit(solution)/shard_map/psum | solution.py:152
  188.5 196.3 %all-reduce.88.cloned.1.call-start = ((), (), s32[]{:S(2)}) async-start(), calls=%async_computation.2 | async-start | bytes 262144 | tf_op jit(solution)/shard_map/psum | solution.py:153
Sparse Core Ops, SparseCore 0:
  118.1 70.3 all-reduce.83
  190.8 137.6 all-reduce.85
  330.8 53.8 all-reduce.87
where the time goes:
time: 393 us
  waiting for transfers between devices  269 us (68%)
  blocking collectives  52.2 us (13%)
  between operations  20.5 us (5%)
  starting transfers between devices  19.7 us (5%)
  other arithmetic  14.9 us (4%)
  matrix products  10.2 us (3%)
  local copies, waits for them, and re-layouts  6.28 us (2%)
    psum x1, waiting for transfers between devices, per_device(): head_grad = lax.psum(head_grad, 'outer')  140 us
    psum x1, waiting for transfers between devices, per_device(): head_grad = lax.psum(grad_local, 'inner')  69.9 us
    psum x1, waiting for transfers between devices, per_device(): head_grad = lax.psum(head_grad, 'take')  55.2 us
    all_gather x2, blocking collectives, exclusive_in_group(): gathered = lax.all_gather(totals, axis)  52.2 us
    ppermute x3, starting transfers between devices, extended_2(): lax.ppermute(lax.slice_in_dim(block, 0, width, axis=dim), axis, backward)  12.2 us
    add x13, other arithmetic, combine(): new_c = a_two * a_two * c_one / denom + c_two  9.96 us
    dot_general x9, matrix products, conv_layer(): jnp.einsum('tfw,wv->tfv', piece, weights[tap], preferred_element_type=jnp...  8.6 us
  transfers between devices with their start and end apart: 9, of which 7 were waited for; matrix products, arithmetic and copies ran while one was open for 2% of the time, Pallas kernels for 0%

commit v1 on v0

--- a/solution.py
+++ b/solution.py
@@ -149,7 +149,7 @@
         "tfw,tfs->ws", hidden, head_cotangent, preferred_element_type=jnp.float32
     )
     head_grad = lax.psum(grad_local, "inner")
-    head_grad = lax.psum(head_grad, "outer")
+    head_grad = lax.all_gather(head_grad, "outer").sum(axis=0)
     head_grad = lax.psum(head_grad, "take")
     return (final[1], head_grad)
 

time: 393 us -> 278 us (0.71)
  waiting for transfers between devices: 269 us -> 158 us
  blocking collectives: 52.2 us -> 44.6 us
    psum x1 -> x0, waiting for transfers between devices: 140 us -> none  [per_device(): head_grad = lax.psum(head_grad, 'outer')]
    all_gather x0 -> x1, waiting for transfers between devices: none -> 44 us  [per_device(): head_grad = lax.all_gather(head_grad, 'outer').sum(axis=0)]
    psum x1, waiting for transfers between devices: 69.9 us -> 56.2 us  [per_device(): head_grad = lax.psum(grad_local, 'inner')]
    all_gather x2, blocking collectives: 52.2 us -> 44.6 us  [exclusive_in_group(): gathered = lax.all_gather(totals, axis)]
  transfers between devices with their start and end apart: 9 -> 9, of which waited for: 7 -> 7; matrix products, arithmetic and copies ran while one was open for 2% -> 8% of each run, Pallas kernels for 0% -> 0%
where the time goes in v1:
time: 278 us; the launch traced here: 277 us
  waiting for transfers between devices  158 us (57%)
  blocking collectives  44.6 us (16%)
  between operations  20.5 us (7%)
  starting transfers between devices  19.7 us (7%)
  other arithmetic  17.2 us (6%)
  matrix products  11.1 us (4%)
  local copies, waits for them, and re-layouts  6.28 us (2%)
    psum x1, waiting for transfers between devices, per_device(): head_grad = lax.psum(grad_local, 'inner')  56.2 us
    psum x1, waiting for transfers between devices, per_device(): head_grad = lax.psum(head_grad, 'take')  53.7 us
    all_gather x2, blocking collectives, exclusive_in_group(): gathered = lax.all_gather(totals, axis)  44.6 us
    all_gather x1, waiting for transfers between devices, per_device(): head_grad = lax.all_gather(head_grad, 'outer').sum(axis=0)  44 us
    ppermute x3, starting transfers between devices, extended_2(): lax.ppermute(lax.slice_in_dim(block, 0, width, axis=dim), axis, backward)  12 us
    add x13, other arithmetic, combine(): new_c = a_two * a_two * c_one / denom + c_two  9.73 us
    dot_general x9, matrix products, conv_layer(): jnp.einsum('tfw,wv->tfv', piece, weights[tap], preferred_element_type=jnp...  9.48 us
    ppermute x3, starting transfers between devices, extended_2(): lax.ppermute(lax.slice_in_dim(block, block.shape[dim] - width, None, axis...  7.34 us
  transfers between devices with their start and end apart: 9, of which 7 were waited for; matrix products, arithmetic and copies ran while one was open for 8% of the time, Pallas kernels for 0%

profile of v1, /device:TPU:2, one launch (start us, length us, event | category | flops | bytes accessed | tf_op | source)
XLA Modules:
  0.0 277.4 jit_solution(17072008989913779285)
XLA Ops:
  8.4 1.9 collective-permute-start.1
  10.3 2.4 collective-permute-start
  14.3 3.0 %fusion.60 = f32[4,512,256]{2,1,0:T(8,128)} fusion(bf16[4,512,256]{2,1,0:T(8,128)(2,1)} %param.13, bf16[3,3,256,256]{3,2,1,0:T(8,128)(2,1)} %param.14), kind=kOutput, calls=%fused_computation.134 | convolution fusion | flops 268435456 | bytes 3276800 | tf_op jit(solution)/shard_map/tfw,wv->tfv/dot_general | solution.py:105
  25.8 1.1 add_convert_fusion.2
  26.9 3.0 %collective-permute-start.2 = (bf16[4,64,256]{2,1,0:T(8,128)(2,1)S(1)}, bf16[4,64,256]{2,1,0:T(8,128)(2,1)S(1)}, u32[]{:S(2)}, u32[]{:S(2)}) collective-permute-start(bf16[4,64,256]{2,1,0:T(8,128)(2,1)S(1)} %get-tuple-element.107), channel_id=1, source_target_pairs={{0,1},{1,2},{2,3},{3,4},{4,5},{5,6},{6,7},{7,8},{8,9},{9,10},{10,1... | collective-permute-start | bytes 393224 | tf_op jit(solution)/shard_map/ppermute | solution.py:16
  30.0 6.3 %collective-permute-start.3 = (bf16[4,64,256]{2,1,0:T(8,128)(2,1)S(1)}, bf16[4,64,256]{2,1,0:T(8,128)(2,1)S(1)}, u32[]{:S(2)}, u32[]{:S(2)}) collective-permute-start(bf16[4,64,256]{2,1,0:T(8,128)(2,1)S(1)} %get-tuple-element.108), channel_id=1, source_target_pairs={{1,0},{2,1},{3,2},{4,3},{5,4},{6,5},{7,6},{8,7},{9,8},{10,9},{11,1... | collective-permute-start | bytes 393224 | tf_op jit(solution)/shard_map/ppermute | solution.py:19
  37.0 1.8 collective-permute-done.3
  40.5 1.9 collective-permute-start.4
  42.4 3.8 %collective-permute-start.5 = (bf16[4,64,256]{2,1,0:T(8,128)(2,1)S(1)}, bf16[4,64,256]{2,1,0:T(8,128)(2,1)S(1)}, u32[]{:S(2)}, u32[]{:S(2)}) collective-permute-start(bf16[4,64,256]{2,1,0:T(8,128)(2,1)S(1)} %get-tuple-element.106), channel_id=1, source_target_pairs={{1,0},{2,1},{3,2},{4,3},{5,4},{6,5},{7,6},{8,7},{9,8},{10,9},{11,1... | collective-permute-start | bytes 393224 | tf_op jit(solution)/shard_map/ppermute | solution.py:19
  46.9 1.8 collective-permute-done.5
  49.2 2.0 add_convert_fusion
  55.6 1.3 divide_add_fusion.12
  56.9 1.3 divide_add_fusion.11
  58.2 1.3 divide_add_fusion.10
  59.5 1.3 divide_add_fusion.9
  60.8 1.3 divide_add_fusion.8
  62.1 1.2 fusion.30
  66.1 13.5 %all-gather = f32[40,4,64]{2,1,0:T(4,128)S(1)} all-gather(f32[5,4,64]{2,1,0:T(4,128)S(1)} %constant_dynamic-update-slice_fusion.3), channel_id=2, replica_groups=mesh['take'=4,'outer'=16,'inner'=8] {'inner'}, dimensions={0}, use_global_device_ids=true | all-gather | bytes 46080 | tf_op jit(solution)/shard_map/all_gather | solution.py:69
  79.8 56.2 %all-reduce.83.cloned.1.call-done = f32[1,256,128]{2,1,0:T(8,128)} async-done(((f32[1,256,128]{2,1,0:T(8,128)}), f32[1,256,128]{2,1,0:T(8,128)}) %all-reduce.83.cloned.1.call-update) | async-done | bytes 131088 | tf_op jit(solution)/shard_map/psum | solution.py:151
  136.3 31.1 %all_gather.17 = f32[16,5,4,64]{3,2,0,1:T(4,128)S(1)} all-gather(f32[1,5,4,64]{3,2,0,1:T(4,128)S(1)} %slice.674), channel_id=1, replica_groups=mesh['take'=4,'outer'=16,'inner'=8] {'outer'}, dimensions={0}, use_global_device_ids=true | all-gather | bytes 87040 | tf_op jit(solution)/shard_map/all_gather | solution.py:69
  168.2 44.0 %all-gather.3.cloned.1.call-done = f32[16,256,128]{2,1,0:T(8,128)} async-done(((f32[1,256,128]{2,1,0:T(8,128)}), f32[16,256,128]{2,1,0:T(8,128)}) %all-gather.3.cloned.1.call-update) | async-done | bytes 2097168 | tf_op jit(solution)/shard_map/all_gather | solution.py:152
  212.2 2.4 reduce_sum.9
  215.6 53.7 %all-reduce.85.cloned.1.call-done = f32[256,128]{1,0:T(8,128)} async-done(((f32[256,128]{1,0:T(8,128)}), f32[256,128]{1,0:T(8,128)}) %all-reduce.85.cloned.1.call-update) | async-done | bytes 131088 | tf_op jit(solution)/shard_map/psum | solution.py:153
  269.3 1.6 copy.266
  (122 shorter events, 17.7 us)
Async XLA Ops:
  7.2 44.1 %copy-start = (bf16[4,512,128]{2,1,0:T(8,128)(2,1)S(1)}, bf16[4,512,128]{2,1,0:T(8,128)(2,1)}, u32[]{:S(2)}) copy-start(bf16[4,512,128]{2,1,0:T(8,128)(2,1)} %param.21) | copy-start | bytes 1572868
  7.2 16.9 %copy-start.1 = (bf16[4,512,256]{2,1,0:T(8,128)(2,1)S(1)}, bf16[4,512,256]{2,1,0:T(8,128)(2,1)}, u32[]{:S(2)}) copy-start(bf16[4,512,256]{2,1,0:T(8,128)(2,1)} %param.13) | copy-start | bytes 3145732
  7.2 10.1 %copy-start.8 = (s32[3]{0:T(128)S(1)}, s32[3]{0:T(128)}, u32[]{:S(2)}) copy-start(s32[3]{0:T(128)} %param.16) | copy-start | bytes 40
  7.2 16.8 %copy-start.7 = (s32[4,512]{1,0:T(4,128)S(1)}, s32[4,512]{1,0:T(4,128)}, u32[]{:S(2)}) copy-start(s32[4,512]{1,0:T(4,128)} %param.18) | copy-start | bytes 24580
  7.2 128.8 %all-reduce.83.cloned.1.call-start = ((), (), s32[]{:S(2)}) async-start(), calls=%async_computation | async-start | bytes 262144 | tf_op jit(solution)/shard_map/psum | solution.py:151
  8.4 15.8 %collective-permute-start.1 = (bf16[4,64,256]{2,1,0:T(8,128)(2,1)S(1)}, bf16[4,64,256]{2,1,0:T(8,128)(2,1)S(1)}, u32[]{:S(2)}, u32[]{:S(2)}) collective-permute-start(bf16[4,64,256]{2,1,0:T(8,128)(2,1)S(1)} %get-tuple-element.109), channel_id=1, source_target_pairs={{1,0},{2,1},{3,2},{4,3},{5,4},{6,5},{7,6},{8,7},{9,8},{10,9},{11,1... | collective-permute-start | bytes 393224 | tf_op jit(solution)/shard_map/ppermute | solution.py:19
  10.3 13.8 %collective-permute-start = (bf16[4,64,256]{2,1,0:T(8,128)(2,1)S(1)}, bf16[4,64,256]{2,1,0:T(8,128)(2,1)S(1)}, u32[]{:S(2)}, u32[]{:S(2)}) collective-permute-start(bf16[4,64,256]{2,1,0:T(8,128)(2,1)S(1)} %get-tuple-element.110), channel_id=1, source_target_pairs={{0,1},{1,2},{2,3},{3,4},{4,5},{5,6},{6,7},{7,8},{8,9},{9,10},{10,1... | collective-permute-start | bytes 393224 | tf_op jit(solution)/shard_map/ppermute | solution.py:16
  17.3 6.9 %copy-start.3 = (bf16[3,3,256,256]{3,2,1,0:T(8,128)(2,1)S(1)}, bf16[3,3,256,256]{3,2,1,0:T(8,128)(2,1)}, u32[]{:S(2)}) copy-start(bf16[3,3,256,256]{3,2,1,0:T(8,128)(2,1)} %param.14) | copy-start | bytes 3538948
  24.2 1.6 copy-start.2
  26.9 10.1 %collective-permute-start.2 = (bf16[4,64,256]{2,1,0:T(8,128)(2,1)S(1)}, bf16[4,64,256]{2,1,0:T(8,128)(2,1)S(1)}, u32[]{:S(2)}, u32[]{:S(2)}) collective-permute-start(bf16[4,64,256]{2,1,0:T(8,128)(2,1)S(1)} %get-tuple-element.107), channel_id=1, source_target_pairs={{0,1},{1,2},{2,3},{3,4},{4,5},{5,6},{6,7},{7,8},{8,9},{9,10},{10,1... | collective-permute-start | bytes 393224 | tf_op jit(solution)/shard_map/ppermute | solution.py:16
  30.0 8.8 %collective-permute-start.3 = (bf16[4,64,256]{2,1,0:T(8,128)(2,1)S(1)}, bf16[4,64,256]{2,1,0:T(8,128)(2,1)S(1)}, u32[]{:S(2)}, u32[]{:S(2)}) collective-permute-start(bf16[4,64,256]{2,1,0:T(8,128)(2,1)S(1)} %get-tuple-element.108), channel_id=1, source_target_pairs={{1,0},{2,1},{3,2},{4,3},{5,4},{6,5},{7,6},{8,7},{9,8},{10,9},{11,1... | collective-permute-start | bytes 393224 | tf_op jit(solution)/shard_map/ppermute | solution.py:19
  40.5 6.4 %collective-permute-start.4 = (bf16[4,64,256]{2,1,0:T(8,128)(2,1)S(1)}, bf16[4,64,256]{2,1,0:T(8,128)(2,1)S(1)}, u32[]{:S(2)}, u32[]{:S(2)}) collective-permute-start(bf16[4,64,256]{2,1,0:T(8,128)(2,1)S(1)} %get-tuple-element.105), channel_id=1, source_target_pairs={{0,1},{1,2},{2,3},{3,4},{4,5},{5,6},{6,7},{7,8},{8,9},{9,10},{10,1... | collective-permute-start | bytes 393224 | tf_op jit(solution)/shard_map/ppermute | solution.py:16
  42.4 6.3 %collective-permute-start.5 = (bf16[4,64,256]{2,1,0:T(8,128)(2,1)S(1)}, bf16[4,64,256]{2,1,0:T(8,128)(2,1)S(1)}, u32[]{:S(2)}, u32[]{:S(2)}) collective-permute-start(bf16[4,64,256]{2,1,0:T(8,128)(2,1)S(1)} %get-tuple-element.106), channel_id=1, source_target_pairs={{1,0},{2,1},{3,2},{4,3},{5,4},{6,5},{7,6},{8,7},{9,8},{10,9},{11,1... | collective-permute-start | bytes 393224 | tf_op jit(solution)/shard_map/ppermute | solution.py:19
  49.2 3.2 %copy-start.4 = (bf16[256,128]{1,0:T(8,128)(2,1)S(1)}, bf16[256,128]{1,0:T(8,128)(2,1)}, u32[]{:S(2)}) copy-start(bf16[256,128]{1,0:T(8,128)(2,1)} %param.17) | copy-start | bytes 196612
  52.4 1.2 copy-start.5
  52.9 159.3 %all-gather.3.cloned.1.call-start = ((), (), s32[]{:S(2)}) async-start(), calls=%async_computation.1 | async-start | bytes 2228224 | tf_op jit(solution)/shard_map/all_gather | solution.py:152
  136.0 133.3 %all-reduce.85.cloned.1.call-start = ((), (), s32[]{:S(2)}) async-start(), calls=%async_computation.2 | async-start | bytes 262144 | tf_op jit(solution)/shard_map/psum | solution.py:153
  136.2 32.0 %copy-start.6 = (f32[1,5,4,64]{3,2,1,0:T(4,128)S(1)}, f32[1,5,4,64]{3,2,1,0:T(4,128)}, u32[]{:S(2)}) copy-start(f32[1,5,4,64]{3,2,1,0:T(4,128)} %constant.139.clone.1) | copy-start | bytes 15364
Sparse Core Ops, SparseCore 0:
  53.0 82.9 all-reduce.82
  138.1 74.0 all-gather.2
  215.1 54.2 all-reduce.84
